TPU v7x, 32 devices: a whole 2x2x4 slice. The times are simulated.
32 devices in a mesh: rep: 4 (over x, core), frame: 4 (over z), row: 2 (over y).
Axes of the slice: x: 2, y: 2, z: 4, core: 2. Of those that a mesh axis runs over, the one named last changes fastest.
Arguments:
- activations: bfloat16 [4, 4, 16, 32, 1280], P('rep', 'frame', 'row'), may hold values from -70 to 70, as said below
- spatial_weight: bfloat16 [9, 1280, 1280], P(None, None, ('rep', 'frame')), may hold values from -0.0546875 to 0.0546875
- temporal_weight: bfloat16 [3, 1280, 1280], P(None, None, ('rep', 'frame')), may hold values from -0.09375 to 0.09375
- first_gain: float32 [1280], replicated, may hold values from 0.25 to 1.75
- first_shift: float32 [1280], replicated, may hold values from -1.5 to 1.5
- spatial_bias: float32 [1280], replicated, may hold values from -2.5 to 2.5
- second_gain: float32 [1280], replicated, may hold values from 0.25 to 1.75
- second_shift: float32 [1280], replicated, may hold values from -1.5 to 1.5
- temporal_bias: float32 [1280], replicated, may hold values from -1.5 to 1.5
Outputs:
- block_out: float32 [4, 4, 16, 32, 1280], P('rep', 'frame', 'row')
Inputs may be any that keep to these rules, and one draw needn't show every extreme that they name: `activations`: finite values.
All inputs are finite; a program needn't handle non-finite values.
Results may differ from a plain program's by a relative error of at most 0.0009.
Values may be sent and summed in bfloat16 or wider, within the bound.
No kernel may reach another device: no remote copies, remote signals or barrier semaphores. Data moves between devices by JAX's collectives and lax.ppermute only.
A program may use at most 128 MiB of HBM per device.

v0:
```python
import jax
import jax.numpy as jnp
from jax import lax
from jax.sharding import PartitionSpec as P

GROUPS = 32
EPS = 1e-05


def padded_2(block, sides, width):
    for axis, dim in sides:
        count = lax.axis_size(axis)
        forward = [(i, i + 1) for i in range(count - 1)]
        backward = [(target, source) for source, target in forward]
        low = lax.ppermute(
            lax.slice_in_dim(block, block.shape[dim] - width, None, axis=dim), axis, forward
        )
        high = lax.ppermute(lax.slice_in_dim(block, 0, width, axis=dim), axis, backward)
        block = jnp.concatenate([low, block, high], axis=dim)
    return block


def norm_silu(field, gain, shift):
    samples = field.shape[0]
    width = field.shape[-1] // GROUPS
    grouped = field.reshape(samples, -1, GROUPS, width)
    sums = jnp.sum(grouped, axis=(1, 3))
    squares = jnp.sum(grouped * grouped, axis=(1, 3))
    sums, squares = lax.psum((sums, squares), ("frame", "row"))
    count = grouped.shape[1] * width * lax.axis_size("frame") * lax.axis_size("row")
    mean = sums / count
    variance = squares / count - mean * mean
    inverse = lax.rsqrt(variance + EPS)
    mean_full = jnp.repeat(mean, width, axis=1)[:, None, None, None, :]
    inverse_full = jnp.repeat(inverse, width, axis=1)[:, None, None, None, :]
    normed = (field - mean_full) * inverse_full * gain + shift
    return jax.nn.silu(normed).astype(jnp.bfloat16)


def conv_taps(padded, weights, rows, cols):
    leading = padded.shape[0] * padded.shape[1]
    channels = padded.shape[-1]
    summed = jnp.zeros((leading * rows * cols, weights.shape[-1]), jnp.float32)
    for row_tap in range(3):
        for col_tap in range(3):
            section = padded[:, :, row_tap : row_tap + rows, col_tap : col_tap + cols, :].reshape(
                -1, channels
            )
            summed = summed + jnp.dot(
                section, weights[3 * row_tap + col_tap], preferred_element_type=jnp.float32
            )
    return summed.reshape(padded.shape[0], padded.shape[1], rows, cols, -1)


def time_taps(window, weights, frames_dev):
    channels = window.shape[-1]
    samples, rows, cols = (window.shape[0], window.shape[2], window.shape[3])
    summed = jnp.zeros((samples * frames_dev * rows * cols, weights.shape[-1]), jnp.float32)
    for tap in range(3):
        section = window[:, tap : tap + frames_dev].reshape(-1, channels)
        summed = summed + jnp.dot(section, weights[tap], preferred_element_type=jnp.float32)
    return summed.reshape(samples, frames_dev, rows, cols, -1)


def shards(
    activations,
    spatial_weight,
    temporal_weight,
    first_gain,
    first_shift,
    spatial_bias,
    second_gain,
    second_shift,
    temporal_bias,
):
    frames_dev = activations.shape[1]
    rows_dev = activations.shape[2]
    cols = activations.shape[3]
    inputs = activations.astype(jnp.float32)
    first = norm_silu(inputs, first_gain, first_shift)
    with_rims = padded_2(first, (("row", 2),), 1)
    gathered = lax.all_gather(with_rims, "rep", axis=0, tiled=True)
    padded = jnp.pad(gathered, ((0, 0), (0, 0), (0, 0), (1, 1), (0, 0)))
    quarter = conv_taps(
        padded, lax.all_gather(spatial_weight, "frame", axis=2, tiled=True), rows_dev, cols
    )
    spatial = lax.all_to_all(
        quarter.astype(jnp.bfloat16), "rep", split_axis=0, concat_axis=4, tiled=True
    ).astype(quarter.dtype)
    spatial = spatial + spatial_bias
    second = norm_silu(spatial, second_gain, second_shift)
    window = padded_2(second, (("frame", 1),), 1)
    window_all = lax.all_gather(window, "rep", axis=0, tiled=True)
    quarter_time = time_taps(
        window_all, lax.all_gather(temporal_weight, "frame", axis=2, tiled=True), frames_dev
    )
    temporal = lax.all_to_all(
        quarter_time.astype(jnp.bfloat16), "rep", split_axis=0, concat_axis=4, tiled=True
    ).astype(quarter_time.dtype)
    return inputs + temporal + temporal_bias


def solution(mesh):
    placed = (
        P("rep", "frame", "row", None, None),
        P(None, None, ("rep", "frame")),
        P(None, None, ("rep", "frame")),
        P(),
        P(),
        P(),
        P(),
        P(),
        P(),
    )
    return jax.shard_map(
        shards,
        mesh=mesh,
        in_specs=placed,
        out_specs=P("rep", "frame", "row", None, None),
        check_vma=False,
    )
```

profile of v0, /device:TPU:0, one launch (start us, length us, event | category | flops | bytes accessed | tf_op | source)
XLA Modules:
  0.0 412.9 jit_solution(1252224786105186306)
XLA Ops:
  6.5 1.3 convert_reduce_fusion
  7.8 0.1 reduce_sum.54
  8.0 0.1 reduce_sum.55
  8.1 0.1 reduce_sum.62
  8.2 23.2 %all-reduce.2 = (f32[1,32]{1,0:T(1,128)S(1)}, f32[1,32]{1,0:T(1,128)S(1)}) all-reduce(f32[1,32]{1,0:T(1,128)S(1)} %bitcast.114, f32[1,32]{1,0:T(1,128)S(1)} %bitcast.112), channel_id=1, replica_groups=mesh['rep'=4,'frame'=4,'row'=2] {'frame','row'}, use_global_device_ids=true, to_apply=%region_5.6 | all-reduce | flops 64 | bytes 512 | tf_op jit(solution)/shard_map/psum | solution.py:29
  31.5 0.1 broadcast_in_dim.27
  31.6 0.1 broadcast_in_dim.29
  31.7 1.6 fusion.14
  33.3 1.3 collective-permute-start
  34.6 1.3 collective-permute-start.1
  35.9 0.7 collective-permute-done
  36.6 4.3 %collective-permute-done.1 = bf16[1,1,1,32,1280]{4,3,2,1,0:T(8,128)(2,1)S(1)} collective-permute-done((bf16[1,1,1,32,1280]{4,3,2,1,0:T(8,128)(2,1)S(1)}, bf16[1,1,1,32,1280]{4,3,2,1,0:T(8,128)(2,1)S(1)}, u32[]{:S(2)}, u32[]{:S(2)}) %collective-permute-start.1) | collective-permute-done | bytes 81952 | tf_op jit(solution)/shard_map/ppermute | solution.py:18
  40.9 1.0 pad_maximum_fusion.1
  42.0 0.7 all-gather.7.cloned.1.call-update
  42.7 26.3 %all-gather.5.cloned.1.call-done = bf16[4,1,10,32,1280]{4,3,2,1,0:T(8,128)(2,1)} async-done(((bf16[1,1,10,32,1280]{4,3,2,1,0:T(8,128)(2,1)}), bf16[4,1,10,32,1280]{4,3,2,1,0:T(8,128)(2,1)}) %all-gather.5.cloned.1.call-update) | async-done | bytes 3276816 | tf_op jit(solution)/shard_map/all_gather | solution.py:82
  69.0 19.4 %pad_slice_fusion = (bf16[4,1,8,32,1280]{4,3,2,1,0:T(8,128)(2,1)S(1)}, bf16[4,1,8,32,1280]{4,3,2,1,0:T(8,128)(2,1)}, bf16[4,1,8,32,1280]{4,3,2,1,0:T(8,128)(2,1)...) fusion(bf16[4,1,10,32,1280]{4,3,2,1,0:T(8,128)(2,1)} %all-gathe, ...), kind=kLoop, calls=%fused_computation | loop fusion | bytes 34734080 | tf_op jit(solution)/shard_map/slice | solution.py:46
  88.3 115.2 %all-gather.7.cloned.1.call-done = bf16[9,1280,320]{1,2,0:T(8,128)(2,1)} async-done(((bf16[9,1280,80]{1,2,0:T(8,128)(2,1)}), bf16[9,1280,320]{1,2,0:T(8,128)(2,1)}) %all-gather.7.cloned.1.call-update) | async-done | bytes 7372816 | tf_op jit(solution)/shard_map/all_gather | solution.py:85
  203.6 3.1 fusion.18
  206.7 3.0 convolution_add_fusion.9
  209.7 1.0 convolution_add_fusion.8
  210.8 0.7 copy-done.5
  211.5 1.0 convolution_add_fusion.7
  212.5 0.7 copy-done.4
  213.2 1.0 convolution_add_fusion.6
  214.3 0.7 copy-done.3
  215.0 1.0 convolution_add_fusion.5
  216.0 0.7 copy-done.2
  216.7 1.0 convolution_add_fusion.4
  217.8 0.7 copy-done.1
  218.4 1.0 convolution_add_fusion.3
  219.5 1.1 fusion.4
  220.6 1.2 copy.24
  221.7 3.5 all-to-all-start
  225.4 11.5 %all-to-all-done = bf16[4,1,8,32,320]{4,3,2,1,0:T(8,128)(2,1)S(1)} async-done(((bf16[4,1,8,32,320]{4,3,2,1,0:T(8,128)(2,1)}), bf16[4,1,8,32,320]{4,3,2,1,0:T(8,128)(2,1)S(1)}, u32[]{:S(2)}, u32[]{:S(2)}) %all-to-all-start) | async-done | bytes 655392 | tf_op jit(solution)/shard_map/all_to_all | solution.py:87
  236.8 0.3 fusion.2
  237.2 0.1 reduce_sum.82
  237.4 0.1 reduce_sum.86
  237.5 18.8 %all-reduce.1 = (f32[1,32]{1,0:T(1,128)S(1)}, f32[1,32]{1,0:T(1,128)S(1)}) all-reduce(f32[1,32]{1,0:T(1,128)S(1)} %bitcast.113, f32[1,32]{1,0:T(1,128)S(1)} %bitcast.111), channel_id=1, replica_groups=mesh['rep'=4,'frame'=4,'row'=2] {'frame','row'}, use_global_device_ids=true, to_apply=%region_11.12 | all-reduce | flops 64 | bytes 512 | tf_op jit(solution)/shard_map/psum | solution.py:29
  256.4 0.1 broadcast_in_dim.31
  256.6 0.1 broadcast_in_dim.33
  256.6 0.2 convert_bitcast_fusion
  256.8 1.0 copy.26
  257.9 0.9 reshape.227
  258.8 0.5 multiply_convert_fusion
  259.3 1.3 collective-permute-start.2
  260.6 1.3 collective-permute-start.3
  261.9 8.9 %collective-permute-done.2 = bf16[1,1,8,32,1280]{4,3,2,1,0:T(8,128)(2,1)S(1)} collective-permute-done((bf16[1,1,8,32,1280]{4,3,2,1,0:T(8,128)(2,1)S(1)}, bf16[1,1,8,32,1280]{4,3,2,1,0:T(8,128)(2,1)S(1)}, u32[]{:S(2)}, u32[]{:S(2)}) %collective-permute-start.2) | collective-permute-done | bytes 655392 | tf_op jit(solution)/shard_map/ppermute | solution.py:15
  270.8 4.2 %collective-permute-done.3 = bf16[1,1,8,32,1280]{4,3,2,1,0:T(8,128)(2,1)S(1)} collective-permute-done((bf16[1,1,8,32,1280]{4,3,2,1,0:T(8,128)(2,1)S(1)}, bf16[1,1,8,32,1280]{4,3,2,1,0:T(8,128)(2,1)S(1)}, u32[]{:S(2)}, u32[]{:S(2)}) %collective-permute-start.3) | collective-permute-done | bytes 655392 | tf_op jit(solution)/shard_map/ppermute | solution.py:18
  274.9 1.6 pad_maximum_fusion
  276.6 0.5 all-gather.11.cloned.1.call-update
  277.1 52.2 %all-gather.9.cloned.1.call-done = bf16[4,3,8,32,1280]{4,3,2,1,0:T(8,128)(2,1)} async-done(((bf16[1,3,8,32,1280]{4,3,2,1,0:T(8,128)(2,1)}), bf16[4,3,8,32,1280]{4,3,2,1,0:T(8,128)(2,1)}) %all-gather.9.cloned.1.call-update) | async-done | bytes 7864336 | tf_op jit(solution)/shard_map/all_gather | solution.py:93
  329.3 5.2 %fusion.19 = (bf16[4,1,8,32,1280]{4,3,2,1,0:T(8,128)(2,1)S(1)}, bf16[4,1,8,32,1280]{4,3,2,1,0:T(8,128)(2,1)}, bf16[4,1,8,32,1280]{4,3,2,1,0:T(8,128)(2,1)}) fusion(bf16[4,3,8,32,1280]{4,3,2,1,0:T(8,128)(2,1)} %all-gather.9.cloned.1.call-done), kind=kLoop, calls=%fused_computation.61 | loop fusion | bytes 15728640 | tf_op jit(solution)/shard_map/slice | solution.py:60
  334.5 48.2 %all-gather.11.cloned.1.call-done = bf16[3,1280,320]{1,2,0:T(8,128)(2,1)} async-done(((bf16[3,1280,80]{1,2,0:T(8,128)(2,1)}), bf16[3,1280,320]{1,2,0:T(8,128)(2,1)}) %all-gather.11.cloned.1.call-update) | async-done | bytes 2457616 | tf_op jit(solution)/shard_map/all_gather | solution.py:95
  382.7 3.1 fusion.17
  385.8 0.4 copy-done.14
  386.2 1.0 convolution_add_fusion.1
  387.3 1.0 fusion.5
  388.3 0.4 copy.27
  388.7 14.2 %all_to_all.8 = bf16[4,1,8,32,320]{4,3,2,1,0:T(8,128)(2,1)S(1)} all-to-all(bf16[4,1,8,32,320]{4,3,2,1,0:T(8,128)(2,1)S(1)} %bitcast.98), channel_id=1, replica_groups=mesh['rep'=4,'frame'=4,'row'=2] {'rep'}, dimensions={0} | all-to-all | bytes 1310720 | tf_op jit(solution)/shard_map/all_to_all | solution.py:97
  402.8 0.2 convert_bitcast_fusion.1
  403.0 1.0 copy.29
  404.1 0.9 reshape.228
  405.0 0.1 copy-done
  405.1 1.2 fusion.16
  (40 shorter events, 0.9 us)
Async XLA Ops:
  6.5 62.4 %all-gather.5.cloned.1.call-start = ((), (), s32[]{:S(2)}) async-start(), calls=%async_computation.2 | async-start | bytes 4096000 | tf_op jit(solution)/shard_map/all_gather | solution.py:82
  33.3 3.3 collective-permute-start
  34.6 6.3 %collective-permute-start.1 = (bf16[1,1,1,32,1280]{4,3,2,1,0:T(8,128)(2,1)S(1)}, bf16[1,1,1,32,1280]{4,3,2,1,0:T(8,128)(2,1)S(1)}, u32[]{:S(2)}, u32[]{:S(2)}) collective-permute-start(bf16[1,1,1,32,1280]{4,3,2,1,0:T(8,128)(2,1)S(1)} %get-tuple-element.26), channel_id=1, source_target_pairs={{1,0},{3,2},{5,4},{7,6},{9,8},{11,10},{13,12},{15,14},{17,16},{19,... | collective-permute-start | bytes 245768 | tf_op jit(solution)/shard_map/ppermute | solution.py:18
  42.0 161.6 %all-gather.7.cloned.1.call-start = ((), (), s32[]{:S(2)}) async-start(), calls=%async_computation.3 | async-start | bytes 9216000 | tf_op jit(solution)/shard_map/all_gather | solution.py:85
  203.6 3.1 copy-start.7
  203.6 6.1 %copy-start.13 = (bf16[9,1280,320]{1,2,0:T(8,128)(2,1)S(1)}, bf16[9,1280,320]{1,2,0:T(8,128)(2,1)}, u32[]{:S(2)}) copy-start(bf16[9,1280,320]{1,2,0:T(8,128)(2,1)} %all-gather.7.cloned.1.call-done) | copy-start | bytes 22118404
  206.7 3.0 copy-start.6
  209.7 1.7 copy-start.5
  211.5 1.7 copy-start.4
  213.2 1.7 copy-start.3
  215.0 1.7 copy-start.2
  216.7 1.7 copy-start.1
  220.6 4.7 %copy-start.9 = (f32[1280]{0:T(1024)S(1)}, f32[1280]{0:T(1024)}, u32[]{:S(2)}) copy-start(f32[1280]{0:T(1024)} %param.14) | copy-start | bytes 15364
  221.7 15.1 %all-to-all-start = ((bf16[4,1,8,32,320]{4,3,2,1,0:T(8,128)(2,1)}), bf16[4,1,8,32,320]{4,3,2,1,0:T(8,128)(2,1)S(1)}, u32[]{:S(2)}, u32[]{:S(2)}) async-start(bf16[4,1,8,32,320]{4,3,2,1,0:T(8,128)(2,1)} %bitcast.23), calls=%async_computation | async-start | bytes 1572864 | tf_op jit(solution)/shard_map/all_to_all | solution.py:87
  225.2 104.1 %all-gather.9.cloned.1.call-start = ((), (), s32[]{:S(2)}) async-start(), calls=%async_computation.4 | async-start | bytes 9830400 | tf_op jit(solution)/shard_map/all_gather | solution.py:93
  257.9 0.9 copy-start.10
  257.9 0.9 copy-start.11
  259.3 11.5 %collective-permute-start.2 = (bf16[1,1,8,32,1280]{4,3,2,1,0:T(8,128)(2,1)S(1)}, bf16[1,1,8,32,1280]{4,3,2,1,0:T(8,128)(2,1)S(1)}, u32[]{:S(2)}, u32[]{:S(2)}) collective-permute-start(bf16[1,1,8,32,1280]{4,3,2,1,0:T(8,128)(2,1)S(1)} %multiply_convert_fusion), channel_id=1, source_target_pairs={{0,2},{2,4},{4,6},{1,3},{3,5},{5,7},{8,10},{10,12},{12,14},{9,11},... | collective-permute-start | bytes 1966088 | tf_op jit(solution)/shard_map/ppermute | solution.py:15
  260.6 14.3 %collective-permute-start.3 = (bf16[1,1,8,32,1280]{4,3,2,1,0:T(8,128)(2,1)S(1)}, bf16[1,1,8,32,1280]{4,3,2,1,0:T(8,128)(2,1)S(1)}, u32[]{:S(2)}, u32[]{:S(2)}) collective-permute-start(bf16[1,1,8,32,1280]{4,3,2,1,0:T(8,128)(2,1)S(1)} %multiply_convert_fusion), channel_id=1, source_target_pairs={{2,0},{4,2},{6,4},{3,1},{5,3},{7,5},{10,8},{12,10},{14,12},{11,9},... | collective-permute-start | bytes 1966088 | tf_op jit(solution)/shard_map/ppermute | solution.py:18
  276.5 106.2 %all-gather.11.cloned.1.call-start = ((), (), s32[]{:S(2)}) async-start(), calls=%async_computation.5 | async-start | bytes 3072000 | tf_op jit(solution)/shard_map/all_gather | solution.py:95
  382.7 3.1 copy-start.8
  382.7 3.5 copy-start.14
  404.1 1.1 copy-start
  404.1 1.1 copy-start.12
Sparse Core Ops, SparseCore 0:
  42.1 26.8 all-gather.4
  70.5 132.9 all-gather.6
  276.7 52.6 all-gather.8
  330.8 51.8 all-gather.10
where the time goes:
time: 413 us
  waiting for transfers between devices  273 us (66%)
  blocking collectives  56.1 us (14%)
  local copies, waits for them, and re-layouts  35 us (8%)
  matrix products  18.6 us (5%)
  between operations  13.5 us (3%)
  starting transfers between devices  8.83 us (2%)
  other arithmetic  8.25 us (2%)
    all_gather x1, waiting for transfers between devices, shards(): lax.all_gather(spatial_weight, 'frame', axis=2, tiled=True)  115 us
    all_gather x1, waiting for transfers between devices, shards(): window_all = lax.all_gather(window, 'rep', axis=0, tiled=True)  52.2 us
    all_gather x1, waiting for transfers between devices, shards(): lax.all_gather(temporal_weight, 'frame', axis=2, tiled=True)  48.2 us
    psum x2, blocking collectives, norm_silu(): sums, squares = lax.psum((sums, squares), ('frame', 'row'))  41.9 us
    all_gather x1, waiting for transfers between devices, shards(): gathered = lax.all_gather(with_rims, 'rep', axis=0, tiled=True)  26.3 us
    slice x1, local copies, waits for them, and re-layouts, conv_taps(): padded[:, :, row_tap:row_tap + rows, col_tap:col_tap + cols, :]  19.4 us
    all_to_all x1, blocking collectives, shards(): lax.all_to_all(quarter_time.astype(jnp.bfloat16), 'rep', split_axis=0, co...  14.2 us
    dot_general x9, matrix products, conv_taps(): jnp.dot(section, weights[3 * row_tap + col_tap], preferred_element_type=j...  13.4 us
  transfers between devices with their start and end apart: 9, of which 9 were waited for; matrix products, arithmetic and copies ran while one was open for 6% of the time, Pallas kernels for 0%

commit v1 on v0

--- a/solution.py
+++ b/solution.py
@@ -5,6 +5,12 @@
 
 GROUPS = 32
 EPS = 1e-05
+
+
+def laid_out(blocks, dim):
+    lengths = list(blocks.shape[1:])
+    lengths[dim] *= blocks.shape[0]
+    return jnp.moveaxis(blocks, 0, dim).reshape(lengths)
 
 
 def padded_2(block, sides, width):
@@ -79,7 +85,19 @@
     inputs = activations.astype(jnp.float32)
     first = norm_silu(inputs, first_gain, first_shift)
     with_rims = padded_2(first, (("row", 2),), 1)
-    gathered = lax.all_gather(with_rims, "rep", axis=0, tiled=True)
+    length = lax.axis_size("rep")
+    pairs = [(i_2, (i_2 + 1) % length) for i_2 in range(length)]
+    back = [(b, a) for a, b in pairs]
+    lower, upper = ([], [])
+    for step in range(length - 1):
+        if step % 2 == 0:
+            lower.append(lax.ppermute(lower[-1] if lower else with_rims, "rep", pairs))
+        else:
+            upper.append(lax.ppermute(upper[-1] if upper else with_rims, "rep", back))
+    pieces = jnp.stack([*lower[::-1], with_rims, *upper])
+    shift_2 = lax.axis_index("rep") - len(lower)
+    pieces = pieces[(jnp.arange(length) - shift_2) % length]
+    gathered = laid_out(pieces, 0)
     padded = jnp.pad(gathered, ((0, 0), (0, 0), (0, 0), (1, 1), (0, 0)))
     quarter = conv_taps(
         padded, lax.all_gather(spatial_weight, "frame", axis=2, tiled=True), rows_dev, cols

time: 413 us -> 355 us (0.86)
  waiting for transfers between devices: 273 us -> 219 us
  local copies, waits for them, and re-layouts: 35 us -> 27.4 us
    all_gather x1, waiting for transfers between devices: 115 us -> 58.6 us  [shards(): lax.all_gather(spatial_weight, 'frame', axis=2, tiled=True)]
    ppermute x0 -> x3, waiting for transfers between devices: none -> 28.8 us  [the longest x2 28.1 us: shards(): lower.append(lax.ppermute(lower[-1] if lower else with_rims, 'rep', pairs))]
    all_gather x1 -> x0, waiting for transfers between devices: 26.3 us -> none  [shards(): gathered = lax.all_gather(with_rims, 'rep', axis=0, tiled=True)]
    slice x1, local copies, waits for them, and re-layouts: 19.4 us -> 8.52 us  [conv_taps(): padded[:, :, row_tap:row_tap + rows, col_tap:col_tap + cols, :]]
  transfers between devices with their start and end apart: 9 -> 11, of which waited for: 9 -> 11; matrix products, arithmetic and copies ran while one was open for 6% -> 6% of each run, Pallas kernels for 0% -> 0%
where the time goes in v1:
time: 355 us
  waiting for transfers between devices  219 us (62%)
  blocking collectives  56.8 us (16%)
  local copies, waits for them, and re-layouts  27.4 us (8%)
  matrix products  18.6 us (5%)
  between operations  13.5 us (4%)
  starting transfers between devices  10.7 us (3%)
  other arithmetic  9.14 us (3%)
    all_gather x1, waiting for transfers between devices, shards(): lax.all_gather(spatial_weight, 'frame', axis=2, tiled=True)  58.6 us
    all_gather x1, waiting for transfers between devices, shards(): window_all = lax.all_gather(window, 'rep', axis=0, tiled=True)  51.6 us
    all_gather x1, waiting for transfers between devices, shards(): lax.all_gather(temporal_weight, 'frame', axis=2, tiled=True)  48.3 us
    psum x2, blocking collectives, norm_silu(): sums, squares = lax.psum((sums, squares), ('frame', 'row'))  42.6 us
    ppermute x2, waiting for transfers between devices, shards(): lower.append(lax.ppermute(lower[-1] if lower else with_rims, 'rep', pairs))  28.1 us
    all_to_all x1, blocking collectives, shards(): lax.all_to_all(quarter_time.astype(jnp.bfloat16), 'rep', split_axis=0, co...  14.2 us
    dot_general x9, matrix products, conv_taps(): jnp.dot(section, weights[3 * row_tap + col_tap], preferred_element_type=j...  13.4 us
    all_to_all x1, waiting for transfers between devices, shards(): lax.all_to_all(quarter.astype(jnp.bfloat16), 'rep', split_axis=0, concat_...  11.5 us
  transfers between devices with their start and end apart: 11, of which 11 were waited for; matrix products, arithmetic and copies ran while one was open for 6% of the time, Pallas kernels for 0%

profile of v1, /device:TPU:0, one launch (start us, length us, event | category | flops | bytes accessed | tf_op | source)
XLA Modules:
  0.0 354.6 jit_solution(11678706592531798918)
XLA Ops:
  6.5 0.7 all-gather.4.cloned.1.call-update
  7.3 1.3 convert_reduce_fusion
  8.7 0.1 reduce_sum.55
  8.9 23.7 %all-reduce.2 = (f32[1,32]{1,0:T(1,128)S(1)}, f32[1,32]{1,0:T(1,128)S(1)}) all-reduce(f32[1,32]{1,0:T(1,128)S(1)} %bitcast.128, f32[1,32]{1,0:T(1,128)S(1)} %bitcast.126), channel_id=1, replica_groups=mesh['rep'=4,'frame'=4,'row'=2] {'frame','row'}, use_global_device_ids=true, to_apply=%region_5.6 | all-reduce | flops 64 | bytes 512 | tf_op jit(solution)/shard_map/psum | solution.py:35
  33.0 0.5 fusion.14
  33.5 1.3 collective-permute-start
  34.8 1.3 collective-permute-start.1
  36.1 0.7 collective-permute-done
  36.9 4.3 %collective-permute-done.1 = bf16[1,1,1,32,1280]{4,3,2,1,0:T(8,128)(2,1)S(1)} collective-permute-done((bf16[1,1,1,32,1280]{4,3,2,1,0:T(8,128)(2,1)S(1)}, bf16[1,1,1,32,1280]{4,3,2,1,0:T(8,128)(2,1)S(1)}, u32[]{:S(2)}, u32[]{:S(2)}) %collective-permute-start.1) | collective-permute-done | bytes 81952 | tf_op jit(solution)/shard_map/ppermute | solution.py:24
  41.2 1.0 fusion.21
  42.2 1.7 collective-permute-start.4
  43.9 17.2 %collective-permute-done.2 = bf16[1,1,10,32,1280]{4,3,2,1,0:T(8,128)(2,1)S(1)} collective-permute-done((bf16[1,1,10,32,1280]{4,3,2,1,0:T(8,128)(2,1)}, bf16[1,1,10,32,1280]{4,3,2,1,0:T(8,128)(2,1)S(1)}, u32[]{:S(2)}, u32[]{:S(2)}) %collective-permute-start.2) | collective-permute-done | bytes 819232 | tf_op jit(solution)/shard_map/ppermute | solution.py:94
  61.1 0.2 collective-permute-start.3
  61.4 0.7 collective-permute-done.4
  62.1 10.9 %collective-permute-done.3 = bf16[1,1,10,32,1280]{4,3,2,1,0:T(8,128)(2,1)S(1)} collective-permute-done((bf16[1,1,10,32,1280]{4,3,2,1,0:T(8,128)(2,1)S(1)}, bf16[1,1,10,32,1280]{4,3,2,1,0:T(8,128)(2,1)S(1)}, u32[]{:S(2)}, u32[]{:S(2)}) %collective-permute-start.3) | collective-permute-done | bytes 819232 | tf_op jit(solution)/shard_map/ppermute | solution.py:94
  72.9 2.0 maximum_bitcast_fusion
  74.9 2.7 gather_fusion
  77.6 8.5 %pad_slice_fusion = (bf16[4,1,8,32,1280]{4,3,2,0,1:T(8,128)(2,1)}, bf16[4,1,8,32,1280]{4,3,2,0,1:T(8,128)(2,1)}, bf16[4,1,8,32,1280]{4,3,2,0,1:T(8,128)(2,1)}, b...) fusion(bf16[4,1,10,32,1280]{4,3,2,0,1:T(8,128)(2,1)S(1)} %bitca, ...), kind=kLoop, calls=%fused_computation.1 | loop fusion | bytes 34734080 | tf_op jit(solution)/shard_map/slice | solution.py:52
  86.1 58.6 %all-gather.4.cloned.1.call-done = bf16[9,1280,320]{1,2,0:T(8,128)(2,1)} async-done(((bf16[9,1280,80]{1,2,0:T(8,128)(2,1)}), bf16[9,1280,320]{1,2,0:T(8,128)(2,1)}) %all-gather.4.cloned.1.call-update) | async-done | bytes 7372816 | tf_op jit(solution)/shard_map/all_gather | solution.py:103
  144.7 3.1 fusion.18
  147.8 3.0 convolution_add_fusion.9
  150.8 1.0 convolution_add_fusion.8
  151.9 0.7 copy-done.7
  152.6 1.0 convolution_add_fusion.7
  153.6 0.7 copy-done.6
  154.3 1.0 convolution_add_fusion.6
  155.4 0.7 copy-done.5
  156.0 1.0 convolution_add_fusion.5
  157.1 0.7 copy-done.4
  157.8 1.0 convolution_add_fusion.4
  158.8 0.7 copy-done.3
  159.5 1.0 convolution_add_fusion.3
  160.6 0.7 copy-done.2
  161.3 1.0 fusion.4
  162.3 1.2 copy.24
  163.5 3.5 all-to-all-start
  167.1 11.5 %all-to-all-done = bf16[4,1,8,32,320]{4,3,2,1,0:T(8,128)(2,1)S(1)} async-done(((bf16[4,1,8,32,320]{4,3,2,1,0:T(8,128)(2,1)}), bf16[4,1,8,32,320]{4,3,2,1,0:T(8,128)(2,1)S(1)}, u32[]{:S(2)}, u32[]{:S(2)}) %all-to-all-start) | async-done | bytes 655392 | tf_op jit(solution)/shard_map/all_to_all | solution.py:105
  178.6 0.3 fusion.2
  179.0 0.1 reduce_sum.82
  179.2 0.1 reduce_sum.86
  179.3 18.9 %all-reduce.1 = (f32[1,32]{1,0:T(1,128)S(1)}, f32[1,32]{1,0:T(1,128)S(1)}) all-reduce(f32[1,32]{1,0:T(1,128)S(1)} %bitcast.127, f32[1,32]{1,0:T(1,128)S(1)} %bitcast.125), channel_id=1, replica_groups=mesh['rep'=4,'frame'=4,'row'=2] {'frame','row'}, use_global_device_ids=true, to_apply=%region_11.12 | all-reduce | flops 64 | bytes 512 | tf_op jit(solution)/shard_map/psum | solution.py:35
  198.5 0.2 convert_bitcast_fusion
  198.7 1.0 copy.26
  199.7 0.9 reshape.280
  200.7 0.5 multiply_convert_fusion
  201.1 1.3 collective-permute-start.5
  202.5 1.3 collective-permute-start.6
  203.8 9.2 %collective-permute-done.5 = bf16[1,1,8,32,1280]{4,3,2,1,0:T(8,128)(2,1)S(1)} collective-permute-done((bf16[1,1,8,32,1280]{4,3,2,1,0:T(8,128)(2,1)S(1)}, bf16[1,1,8,32,1280]{4,3,2,1,0:T(8,128)(2,1)S(1)}, u32[]{:S(2)}, u32[]{:S(2)}) %collective-permute-start.5) | collective-permute-done | bytes 655392 | tf_op jit(solution)/shard_map/ppermute | solution.py:21
  213.0 4.2 %collective-permute-done.6 = bf16[1,1,8,32,1280]{4,3,2,1,0:T(8,128)(2,1)S(1)} collective-permute-done((bf16[1,1,8,32,1280]{4,3,2,1,0:T(8,128)(2,1)S(1)}, bf16[1,1,8,32,1280]{4,3,2,1,0:T(8,128)(2,1)S(1)}, u32[]{:S(2)}, u32[]{:S(2)}) %collective-permute-start.6) | collective-permute-done | bytes 655392 | tf_op jit(solution)/shard_map/ppermute | solution.py:24
  217.1 1.6 pad_maximum_fusion
  218.7 0.7 all-gather.8.cloned.1.call-update
  219.4 51.6 %all-gather.6.cloned.1.call-done = bf16[4,3,8,32,1280]{4,3,2,1,0:T(8,128)(2,1)} async-done(((bf16[1,3,8,32,1280]{4,3,2,1,0:T(8,128)(2,1)}), bf16[4,3,8,32,1280]{4,3,2,1,0:T(8,128)(2,1)}) %all-gather.6.cloned.1.call-update) | async-done | bytes 7864336 | tf_op jit(solution)/shard_map/all_gather | solution.py:111
  271.1 5.2 %fusion.22 = (bf16[4,1,8,32,1280]{4,3,2,1,0:T(8,128)(2,1)S(1)}, bf16[4,1,8,32,1280]{4,3,2,1,0:T(8,128)(2,1)}, bf16[4,1,8,32,1280]{4,3,2,1,0:T(8,128)(2,1)}) fusion(bf16[4,3,8,32,1280]{4,3,2,1,0:T(8,128)(2,1)} %all-gather.6.cloned.1.call-done), kind=kLoop, calls=%fused_computation.71 | loop fusion | bytes 15728640 | tf_op jit(solution)/shard_map/slice | solution.py:66
  276.3 48.3 %all-gather.8.cloned.1.call-done = bf16[3,1280,320]{1,2,0:T(8,128)(2,1)} async-done(((bf16[3,1280,80]{1,2,0:T(8,128)(2,1)}), bf16[3,1280,320]{1,2,0:T(8,128)(2,1)}) %all-gather.8.cloned.1.call-update) | async-done | bytes 2457616 | tf_op jit(solution)/shard_map/all_gather | solution.py:113
  324.6 3.1 fusion.17
  327.7 0.4 copy-done.18
  328.1 1.0 convolution_add_fusion.1
  329.1 1.1 fusion.5
  330.2 0.4 copy.27
  330.6 14.2 %all_to_all.8 = bf16[4,1,8,32,320]{4,3,2,1,0:T(8,128)(2,1)S(1)} all-to-all(bf16[4,1,8,32,320]{4,3,2,1,0:T(8,128)(2,1)S(1)} %bitcast.109), channel_id=1, replica_groups=mesh['rep'=4,'frame'=4,'row'=2] {'rep'}, dimensions={0} | all-to-all | bytes 1310720 | tf_op jit(solution)/shard_map/all_to_all | solution.py:115
  344.7 0.2 convert_bitcast_fusion.1
  344.9 1.0 copy.29
  346.0 0.9 reshape.281
  346.9 1.2 fusion.16
  (55 shorter events, 1.4 us)
Async XLA Ops:
  6.5 26.5 %copy-start = (bf16[1,1,8,32,1280]{4,3,2,1,0:T(8,128)(2,1)S(1)}, bf16[1,1,8,32,1280]{4,3,2,1,0:T(8,128)(2,1)}, u32[]{:S(2)}) copy-start(bf16[1,1,8,32,1280]{4,3,2,1,0:T(8,128)(2,1)} %param.9) | copy-start | bytes 1966084
  6.5 26.5 %copy-start.13 = (f32[1280]{0:T(1024)S(1)}, f32[1280]{0:T(1024)}, u32[]{:S(2)}) copy-start(f32[1280]{0:T(1024)} %param.12) | copy-start | bytes 15364
  6.5 26.5 %copy-start.12 = (f32[1280]{0:T(1024)S(1)}, f32[1280]{0:T(1024)}, u32[]{:S(2)}) copy-start(f32[1280]{0:T(1024)} %param.13) | copy-start | bytes 15364
  6.5 138.1 %all-gather.4.cloned.1.call-start = ((), (), s32[]{:S(2)}) async-start(), calls=%async_computation.2 | async-start | bytes 9216000 | tf_op jit(solution)/shard_map/all_gather | solution.py:103
  33.5 3.3 collective-permute-start
  34.8 6.3 %collective-permute-start.1 = (bf16[1,1,1,32,1280]{4,3,2,1,0:T(8,128)(2,1)S(1)}, bf16[1,1,1,32,1280]{4,3,2,1,0:T(8,128)(2,1)S(1)}, u32[]{:S(2)}, u32[]{:S(2)}) collective-permute-start(bf16[1,1,1,32,1280]{4,3,2,1,0:T(8,128)(2,1)S(1)} %get-tuple-element.28), channel_id=1, source_target_pairs={{1,0},{3,2},{5,4},{7,6},{9,8},{11,10},{13,12},{15,14},{17,16},{19,... | collective-permute-start | bytes 245768 | tf_op jit(solution)/shard_map/ppermute | solution.py:24
  42.2 19.0 %collective-permute-start.2 = (bf16[1,1,10,32,1280]{4,3,2,1,0:T(8,128)(2,1)}, bf16[1,1,10,32,1280]{4,3,2,1,0:T(8,128)(2,1)S(1)}, u32[]{:S(2)}, u32[]{:S(2)}) collective-permute-start(bf16[1,1,10,32,1280]{4,3,2,1,0:T(8,128)(2,1)} %get-tuple-element.26), channel_id=1, source_target_pairs={{0,8},{8,16},{16,24},{24,0},{1,9},{9,17},{17,25},{25,1},{2,10},{10... | collective-permute-start | bytes 2457608 | tf_op jit(solution)/shard_map/ppermute | solution.py:94
  42.2 19.9 %collective-permute-start.4 = (bf16[1,1,10,32,1280]{4,3,2,1,0:T(8,128)(2,1)}, bf16[1,1,10,32,1280]{4,3,2,1,0:T(8,128)(2,1)S(1)}, u32[]{:S(2)}, u32[]{:S(2)}) collective-permute-start(bf16[1,1,10,32,1280]{4,3,2,1,0:T(8,128)(2,1)} %get-tuple-element.26), channel_id=1, source_target_pairs={{8,0},{16,8},{24,16},{0,24},{9,1},{17,9},{25,17},{1,25},{10,2},{18... | collective-permute-start | bytes 2457608 | tf_op jit(solution)/shard_map/ppermute | solution.py:96
  61.1 11.8 %collective-permute-start.3 = (bf16[1,1,10,32,1280]{4,3,2,1,0:T(8,128)(2,1)S(1)}, bf16[1,1,10,32,1280]{4,3,2,1,0:T(8,128)(2,1)S(1)}, u32[]{:S(2)}, u32[]{:S(2)}) collective-permute-start(bf16[1,1,10,32,1280]{4,3,2,1,0:T(8,128)(2,1)S(1)} %collective-permute-done.2), channel_id=1, source_target_pairs={{0,8},{8,16},{16,24},{24,0},{1,9},{9,17},{17,25},{25,1},{2,10},{10... | collective-permute-start | bytes 2457608 | tf_op jit(solution)/shard_map/ppermute | solution.py:94
  144.7 3.1 copy-start.9
  144.7 6.1 %copy-start.17 = (bf16[9,1280,320]{1,2,0:T(8,128)(2,1)S(1)}, bf16[9,1280,320]{1,2,0:T(8,128)(2,1)}, u32[]{:S(2)}) copy-start(bf16[9,1280,320]{1,2,0:T(8,128)(2,1)} %all-gather.4.cloned.1.call-done) | copy-start | bytes 22118404
  147.8 3.0 copy-start.8
  150.8 1.7 copy-start.7
  152.6 1.7 copy-start.6
  154.3 1.7 copy-start.5
  156.0 1.7 copy-start.4
  157.8 1.7 copy-start.3
  159.5 1.7 copy-start.2
  162.3 4.7 %copy-start.11 = (f32[1280]{0:T(1024)S(1)}, f32[1280]{0:T(1024)}, u32[]{:S(2)}) copy-start(f32[1280]{0:T(1024)} %param.14) | copy-start | bytes 15364
  163.5 15.1 %all-to-all-start = ((bf16[4,1,8,32,320]{4,3,2,1,0:T(8,128)(2,1)}), bf16[4,1,8,32,320]{4,3,2,1,0:T(8,128)(2,1)S(1)}, u32[]{:S(2)}, u32[]{:S(2)}) async-start(bf16[4,1,8,32,320]{4,3,2,1,0:T(8,128)(2,1)} %bitcast.30), calls=%async_computation | async-start | bytes 1572864 | tf_op jit(solution)/shard_map/all_to_all | solution.py:105
  167.0 104.1 %all-gather.6.cloned.1.call-start = ((), (), s32[]{:S(2)}) async-start(), calls=%async_computation.3 | async-start | bytes 9830400 | tf_op jit(solution)/shard_map/all_gather | solution.py:111
  198.7 2.0 copy-start.14
  198.7 2.0 copy-start.15
  201.1 11.8 %collective-permute-start.5 = (bf16[1,1,8,32,1280]{4,3,2,1,0:T(8,128)(2,1)S(1)}, bf16[1,1,8,32,1280]{4,3,2,1,0:T(8,128)(2,1)S(1)}, u32[]{:S(2)}, u32[]{:S(2)}) collective-permute-start(bf16[1,1,8,32,1280]{4,3,2,1,0:T(8,128)(2,1)S(1)} %multiply_convert_fusion), channel_id=1, source_target_pairs={{0,2},{2,4},{4,6},{1,3},{3,5},{5,7},{8,10},{10,12},{12,14},{9,11},... | collective-permute-start | bytes 1966088 | tf_op jit(solution)/shard_map/ppermute | solution.py:21
  202.5 14.6 %collective-permute-start.6 = (bf16[1,1,8,32,1280]{4,3,2,1,0:T(8,128)(2,1)S(1)}, bf16[1,1,8,32,1280]{4,3,2,1,0:T(8,128)(2,1)S(1)}, u32[]{:S(2)}, u32[]{:S(2)}) collective-permute-start(bf16[1,1,8,32,1280]{4,3,2,1,0:T(8,128)(2,1)S(1)} %multiply_convert_fusion), channel_id=1, source_target_pairs={{2,0},{4,2},{6,4},{3,1},{5,3},{7,5},{10,8},{12,10},{14,12},{11,9},... | collective-permute-start | bytes 1966088 | tf_op jit(solution)/shard_map/ppermute | solution.py:24
  218.7 105.9 %all-gather.8.cloned.1.call-start = ((), (), s32[]{:S(2)}) async-start(), calls=%async_computation.4 | async-start | bytes 3072000 | tf_op jit(solution)/shard_map/all_gather | solution.py:113
  324.6 3.1 copy-start.10
  324.6 3.5 copy-start.18
  344.9 2.0 copy-start.1
  344.9 2.0 copy-start.16
Sparse Core Ops, SparseCore 0:
  8.9 135.7 all-gather.3
  218.8 52.2 all-gather.5
  272.6 51.8 all-gather.7
